TPU v7x, 256 devices: a whole 4x4x8 slice. The times are simulated.
256 devices in a mesh: dp: 32 (over z, y), tensor: 8 (over x, core).
Axes of the slice: x: 4, y: 4, z: 8, core: 2. Of those that a mesh axis runs over, the one named last changes fastest.
Arguments:
- tokens: bfloat16 [4096, 4096], P('dp', 'tensor'), may hold values from -6 to 6
- grad_out: bfloat16 [4096, 4096], P('dp', 'tensor'), may hold values from -6 to 6
- gate_blocks: int32 [8, 32], P('tensor'), may hold values from -1 to 447, as said below
- gate_values: bfloat16 [8, 32, 128, 128], P('tensor'), may hold values from -0.375 to 0.375
- up_blocks: int32 [8, 32], P('tensor'), may hold values from -1 to 447, as said below
- up_values: bfloat16 [8, 32, 128, 128], P('tensor'), may hold values from -0.375 to 0.375
- down_blocks: int32 [8, 32], P('tensor'), may hold values from -1 to 447, as said below
- down_values: bfloat16 [8, 32, 128, 128], P('tensor'), may hold values from -0.1875 to 0.1875
Outputs:
- mixed: bfloat16 [4096, 4096], P('dp', 'tensor')
- grad_tokens: bfloat16 [4096, 4096], P('dp', 'tensor')
- grad_gate: float32 [8, 32, 128, 128], P('tensor', 'dp')
- grad_up: float32 [8, 32, 128, 128], P('tensor', 'dp')
- grad_down: float32 [8, 32, 128, 128], P('tensor', 'dp')
Inputs may be any that keep to these rules, and one draw needn't show every extreme that they name: `gate_blocks`: each row lists distinct block numbers of one tensor shard in its first slots and -1 in the rest; a row has 16 to 32 listed blocks, one row has exactly 32 and another exactly 16. `up_blocks`: as for gate_blocks, drawn apart. `down_blocks`: as for gate_blocks, drawn apart.
All inputs are finite; a program needn't handle non-finite values.
Results may differ from a plain program's by a relative error of at most 0.015.
Values may be sent and summed in bfloat16 or wider, within the bound.
No kernel may reach another device: no remote copies, remote signals or barrier semaphores. Data moves between devices by JAX's collectives and lax.ppermute only.
A program may use at most 64 MiB of HBM per device.

v0:
```python
import jax
import jax.numpy as jnp
from jax import lax
from jax.sharding import PartitionSpec as P

FF = 14336


def locate(blocks, feature_count):
    flat = blocks[0]
    weight = (flat >= 0).astype(jnp.float32)
    safe = jnp.maximum(flat, 0)
    return (safe // feature_count, safe % feature_count, weight)


def one_hot(targets, weight, count):
    return (targets[:, None] == jnp.arange(count)[None, :]).astype(jnp.float32) * weight[:, None]


def spread(product, table):
    return jnp.einsum("tsn,sc->tcn", product, table, precision=lax.Precision.HIGHEST)


def select(source, position):
    return jnp.take(source, position, axis=1)


def forward_blocks(rows_in, values):
    return jnp.einsum("tsk,skn->tsn", rows_in, values, preferred_element_type=jnp.float32)


def backward_blocks(rows_in, values):
    return jnp.einsum("tsn,skn->tsk", rows_in, values, preferred_element_type=jnp.float32)


def slot_term(left, right, weight):
    product = jnp.einsum("tsk,tsn->skn", left, right, preferred_element_type=jnp.float32)
    return product * weight[:, None, None]


def body(
    tokens, grad_out, gate_blocks, gate_values, up_blocks, up_values, down_blocks, down_values
):
    gathered_x, gathered_dy = (
        lax.all_gather(tokens, "tensor", axis=1, tiled=True),
        lax.all_gather(grad_out, "tensor", axis=1, tiled=True),
    )
    tok_rows, feature_width = gathered_x.shape
    block_size = gate_values.shape[-1]
    feature_count = feature_width // block_size
    hidden_count = FF // (block_size * lax.axis_size("tensor"))
    inputs = gathered_x.reshape(tok_rows, feature_count, block_size)
    upstream = gathered_dy.reshape(tok_rows, feature_count, block_size)
    gate_hid, gate_feat, gate_live = locate(gate_blocks, feature_count)
    up_hid, up_feat, up_live = locate(up_blocks, feature_count)
    down_hid, down_feat, down_live = locate(down_blocks, feature_count)
    gate_rows = select(inputs, gate_feat)
    up_rows = select(inputs, up_feat)
    gate_pre = spread(
        forward_blocks(gate_rows, gate_values[0]), one_hot(gate_hid, gate_live, hidden_count)
    )
    up_pre = spread(forward_blocks(up_rows, up_values[0]), one_hot(up_hid, up_live, hidden_count))
    sigma_gate = jax.nn.sigmoid(gate_pre)
    activated = gate_pre * sigma_gate
    hidden = (activated * up_pre).astype(jnp.bfloat16)
    hidden_rows = select(hidden, down_hid)
    mixed_part = spread(
        forward_blocks(hidden_rows, down_values[0]), one_hot(down_feat, down_live, feature_count)
    )
    mixed_part = mixed_part.reshape(tok_rows, feature_width)
    upstream_rows = select(upstream, down_feat)
    mixed = lax.psum_scatter(
        mixed_part.astype(jnp.bfloat16), "tensor", scatter_dimension=1, tiled=True
    )
    hidden_grad = spread(
        backward_blocks(upstream_rows, down_values[0]), one_hot(down_hid, down_live, hidden_count)
    )
    gate_delta = (hidden_grad * up_pre * sigma_gate * (1.0 + gate_pre * (1.0 - sigma_gate))).astype(
        jnp.bfloat16
    )
    up_delta = (hidden_grad * activated).astype(jnp.bfloat16)
    gate_delta_rows = select(gate_delta, gate_hid)
    up_delta_rows = select(up_delta, up_hid)
    input_part = spread(
        backward_blocks(gate_delta_rows, gate_values[0]),
        one_hot(gate_feat, gate_live, feature_count),
    )
    input_part = input_part + spread(
        backward_blocks(up_delta_rows, up_values[0]), one_hot(up_feat, up_live, feature_count)
    )
    input_part = input_part.reshape(tok_rows, feature_width)
    gate_term = slot_term(gate_rows, gate_delta_rows, gate_live)
    up_term = slot_term(up_rows, up_delta_rows, up_live)
    down_term = slot_term(hidden_rows, upstream_rows, down_live)
    grad_gate, grad_up, grad_down = (
        lax.psum_scatter(term.astype(jnp.bfloat16), "dp", scatter_dimension=0, tiled=True).astype(
            jnp.float32
        )[None]
        for term in (gate_term, up_term, down_term)
    )
    grad_tokens = lax.psum_scatter(
        input_part.astype(jnp.bfloat16), "tensor", scatter_dimension=1, tiled=True
    )
    return (mixed, grad_tokens, grad_gate, grad_up, grad_down)


def solution(mesh):
    in_specs = (
        P("dp", "tensor"),
        P("dp", "tensor"),
        P("tensor", None),
        P("tensor", None, None, None),
        P("tensor", None),
        P("tensor", None, None, None),
        P("tensor", None),
        P("tensor", None, None, None),
    )
    out_specs = (
        P("dp", "tensor"),
        P("dp", "tensor"),
        P("tensor", "dp", None, None),
        P("tensor", "dp", None, None),
        P("tensor", "dp", None, None),
    )
    return jax.shard_map(body, mesh=mesh, in_specs=in_specs, out_specs=out_specs, check_vma=False)
```

profile of v0, /device:TPU:8, one launch (start us, length us, event | category | flops | bytes accessed | tf_op | source)
XLA Modules:
  0.0 825.7 jit_solution(16852433310537458351)
XLA Ops:
  7.2 1.7 copy.39
  9.0 1.7 copy.47
  14.9 24.2 %all-gather.3.cloned.1.call-done = bf16[128,4096]{0,1:T(8,128)(2,1)} async-done(((bf16[128,512]{0,1:T(8,128)(2,1)}), bf16[128,4096]{0,1:T(8,128)(2,1)}) %all-gather.3.cloned.1.call-update) | async-done | bytes 1048592 | tf_op jit(solution)/shard_map/all_gather | solution.py:45
  40.7 26.5 %all-gather.5.cloned.1.call-done = bf16[128,4096]{0,1:T(8,128)(2,1)} async-done(((bf16[128,512]{0,1:T(8,128)(2,1)}), bf16[128,4096]{0,1:T(8,128)(2,1)}) %all-gather.5.cloned.1.call-update) | async-done | bytes 1048592 | tf_op jit(solution)/shard_map/all_gather | solution.py:46
  67.2 2.3 copy.48
  71.2 1.7 gather_fusion
  72.8 3.0 gather_fusion.3
  76.3 2.2 fusion.10
  79.1 2.2 fusion.8
  82.3 2.2 fusion.4
  85.6 1.7 gather_fusion.4
  87.2 3.2 multiply_convert_fusion.2
  90.7 1.7 gather_fusion.2
  92.4 3.2 multiply_convert_fusion
  97.3 3.3 multiply_convert_fusion.1
  101.2 3.0 fusion.14
  105.7 2.3 convolution_bitcast_fusion
  108.9 3.0 fusion
  111.9 3.1 add_convert_fusion
  116.5 190.5 %reduce-scatter.10.cloned.1.call-done = bf16[1,128,128]{2,1,0:T(8,128)(2,1)} async-done(((bf16[32,128,128]{2,1,0:T(8,128)(2,1)}), bf16[1,128,128]{2,1,0:T(8,128)(2,1)}) %reduce-scatter.10.cloned.1.call-update) | async-done | bytes 32784 | tf_op jit(solution)/shard_map/reduce_scatter | solution.py:96
  308.4 217.8 %reduce-scatter.14.cloned.1.call-done = bf16[1,128,128]{2,1,0:T(8,128)(2,1)} async-done(((bf16[32,128,128]{2,1,0:T(8,128)(2,1)}), bf16[1,128,128]{2,1,0:T(8,128)(2,1)}) %reduce-scatter.14.cloned.1.call-update) | async-done | bytes 32784 | tf_op jit(solution)/shard_map/reduce_scatter | solution.py:96
  527.6 217.8 %reduce-scatter.12.cloned.1.call-done = bf16[1,128,128]{2,1,0:T(8,128)(2,1)} async-done(((bf16[32,128,128]{2,1,0:T(8,128)(2,1)}), bf16[1,128,128]{2,1,0:T(8,128)(2,1)}) %reduce-scatter.12.cloned.1.call-update) | async-done | bytes 32784 | tf_op jit(solution)/shard_map/reduce_scatter | solution.py:96
  746.8 35.4 %reduce-scatter.6.cloned.1.call-done = bf16[128,512]{1,0:T(8,128)(2,1)} async-done(((bf16[128,4096]{1,0:T(8,128)(2,1)}), bf16[128,512]{1,0:T(8,128)(2,1)}) %reduce-scatter.6.cloned.1.call-update) | async-done | bytes 131088 | tf_op jit(solution)/shard_map/reduce_scatter | solution.py:72
  782.2 36.7 %reduce-scatter.8.cloned.1.call-done = bf16[128,512]{1,0:T(8,128)(2,1)} async-done(((bf16[128,4096]{1,0:T(8,128)(2,1)}), bf16[128,512]{1,0:T(8,128)(2,1)}) %reduce-scatter.8.cloned.1.call-update) | async-done | bytes 131088 | tf_op jit(solution)/shard_map/reduce_scatter | solution.py:101
  (64 shorter events, 20.9 us)
Async XLA Ops:
  7.2 74.2 %copy-start = (bf16[1,32,128,128]{3,2,1,0:T(8,128)(2,1)S(1)}, bf16[1,32,128,128]{3,2,1,0:T(8,128)(2,1)}, u32[]{:S(2)}) copy-start(bf16[1,32,128,128]{3,2,1,0:T(8,128)(2,1)} %param.19) | copy-start | bytes 3145732
  7.2 31.9 %all-gather.3.cloned.1.call-start = ((), (), s32[]{:S(2)}) async-start(), calls=%async_computation.5 | async-start | bytes 1179648 | tf_op jit(solution)/shard_map/all_gather | solution.py:45
  9.0 58.3 %all-gather.5.cloned.1.call-start = ((), (), s32[]{:S(2)}) async-start(), calls=%async_computation.7 | async-start | bytes 1179648 | tf_op jit(solution)/shard_map/all_gather | solution.py:46
  10.7 296.2 %reduce-scatter.10.cloned.1.call-start = ((), (), s32[]{:S(2)}) async-start(), calls=%async_computation.9 | async-start | bytes 1081344 | tf_op jit(solution)/shard_map/reduce_scatter | solution.py:96
  71.2 4.6 copy-start.2
  72.8 3.0 copy-start.8
  76.3 2.3 copy-start.1
  76.3 2.3 copy-start.5
  79.1 2.3 copy-start.6
  90.5 435.7 %reduce-scatter.14.cloned.1.call-start = ((), (), s32[]{:S(2)}) async-start(), calls=%async_computation.11 | async-start | bytes 1081344 | tf_op jit(solution)/shard_map/reduce_scatter | solution.py:96
  95.6 649.8 %reduce-scatter.12.cloned.1.call-start = ((), (), s32[]{:S(2)}) async-start(), calls=%async_computation.10 | async-start | bytes 1081344 | tf_op jit(solution)/shard_map/reduce_scatter | solution.py:96
  97.3 3.4 copy-start.7
  100.6 681.5 %reduce-scatter.6.cloned.1.call-start = ((), (), s32[]{:S(2)}) async-start(), calls=%async_computation.6 | async-start | bytes 1179648 | tf_op jit(solution)/shard_map/reduce_scatter | solution.py:72
  105.6 2.3 copy-start.3
  105.6 713.2 %reduce-scatter.8.cloned.1.call-start = ((), (), s32[]{:S(2)}) async-start(), calls=%async_computation.8 | async-start | bytes 1179648 | tf_op jit(solution)/shard_map/reduce_scatter | solution.py:101
  105.7 2.3 copy-start.4
Sparse Core Ops, SparseCore 0:
  10.4 28.6 all-gather.2
  41.5 25.6 all-gather.4
  90.6 216.3 reduce-scatter.9
  310.6 215.4 reduce-scatter.13
  529.8 215.5 reduce-scatter.11
  748.4 33.7 reduce-scatter.5
  785.3 33.5 reduce-scatter.7
where the time goes:
time: 826 us
  waiting for transfers between devices  749 us (91%)
  matrix products  31 us (4%)
  local copies, waits for them, and re-layouts  21.4 us (3%)
  between operations  14.4 us (2%)
  other arithmetic  9.27 us (1%)
    reduce_scatter x3, waiting for transfers between devices, body(): lax.psum_scatter(term.astype(jnp.bfloat16), 'dp', scatter_dimension=0, ti...  626 us
    reduce_scatter x1, waiting for transfers between devices, body(): lax.psum_scatter(input_part.astype(jnp.bfloat16), 'tensor', scatter_dimen...  36.7 us
    reduce_scatter x1, waiting for transfers between devices, body(): lax.psum_scatter(mixed_part.astype(jnp.bfloat16), 'tensor', scatter_dimen...  35.4 us
    all_gather x1, waiting for transfers between devices, body(): lax.all_gather(grad_out, 'tensor', axis=1, tiled=True)  26.5 us
    all_gather x1, waiting for transfers between devices, body(): lax.all_gather(tokens, 'tensor', axis=1, tiled=True)  24.2 us
  transfers between devices with their start and end apart: 7, of which 7 were waited for; matrix products, arithmetic and copies ran while one was open for 4% of the time, Pallas kernels for 0%

commit v1 on v0

--- a/solution.py
+++ b/solution.py
@@ -4,6 +4,27 @@
 from jax.sharding import PartitionSpec as P
 
 FF = 14336
+
+
+def gather_around(shard, axis, dim):
+    devices, index, width = (lax.axis_size(axis), lax.axis_index(axis), shard.shape[dim])
+    right = [(i, (i + 1) % devices) for i in range(devices)]
+    downward = [(i, (i - 1) % devices) for i in range(devices)]
+    whole = jnp.zeros((*shard.shape[:dim], devices * width, *shard.shape[dim + 1 :]), shard.dtype)
+    whole = lax.dynamic_update_slice_in_dim(whole, shard, index * width, axis=dim)
+    from_left = from_right = shard
+    half = devices // 2
+    for step in range(1, half + 1):
+        from_left = lax.ppermute(from_left, axis, right)
+        whole = lax.dynamic_update_slice_in_dim(
+            whole, from_left, (index - step) % devices * width, axis=dim
+        )
+        if step < devices - half:
+            from_right = lax.ppermute(from_right, axis, downward)
+            whole = lax.dynamic_update_slice_in_dim(
+                whole, from_right, (index + step) % devices * width, axis=dim
+            )
+    return whole
 
 
 def locate(blocks, feature_count):
@@ -42,7 +63,7 @@
     tokens, grad_out, gate_blocks, gate_values, up_blocks, up_values, down_blocks, down_values
 ):
     gathered_x, gathered_dy = (
-        lax.all_gather(tokens, "tensor", axis=1, tiled=True),
+        gather_around(tokens, "tensor", 1),
         lax.all_gather(grad_out, "tensor", axis=1, tiled=True),
     )
     tok_rows, feature_width = gathered_x.shape

time: 826 us -> 800 us (0.969)
  waiting for transfers between devices: 749 us -> 712 us
  starting transfers between devices: 0.47 us -> 9.52 us
    all_gather x1, waiting for transfers between devices: 26.5 us -> 0.01 us  [body(): lax.all_gather(grad_out, 'tensor', axis=1, tiled=True)]
    all_gather x1 -> x0, waiting for transfers between devices: 24.2 us -> none  [body(): lax.all_gather(tokens, 'tensor', axis=1, tiled=True)]
    ppermute x0 -> x7, waiting for transfers between devices: none -> 11.6 us  [the longest x4 11.2 us: gather_around(): from_left = lax.ppermute(from_left, axis, right)]
    ppermute x0 -> x7, starting transfers between devices: none -> 8.87 us  [the longest x3 8.83 us: gather_around(): from_right = lax.ppermute(from_right, axis, downward)]
  transfers between devices with their start and end apart: 7 -> 13, of which waited for: 7 -> 9; matrix products, arithmetic and copies ran while one was open for 4% -> 6% of each run, Pallas kernels for 0% -> 0%
where the time goes in v1:
time: 800 us; the launch traced here: 799 us
  waiting for transfers between devices  712 us (89%)
  matrix products  34 us (4%)
  local copies, waits for them, and re-layouts  20.7 us (3%)
  between operations  14.6 us (2%)
  starting transfers between devices  9.52 us (1%)
  other arithmetic  8.62 us (1%)
    reduce_scatter x3, waiting for transfers between devices, body(): lax.psum_scatter(term.astype(jnp.bfloat16), 'dp', scatter_dimension=0, ti...  628 us
    reduce_scatter x1, waiting for transfers between devices, body(): lax.psum_scatter(mixed_part.astype(jnp.bfloat16), 'tensor', scatter_dimen...  36.6 us
    reduce_scatter x1, waiting for transfers between devices, body(): lax.psum_scatter(input_part.astype(jnp.bfloat16), 'tensor', scatter_dimen...  35.5 us
    dot_general x6, matrix products, spread(): jnp.einsum('tsn,sc->tcn', product, table, precision=lax.Precision.HIGHEST)  17.8 us
  transfers between devices with their start and end apart: 13, of which 9 were waited for; matrix products, arithmetic and copies ran while one was open for 6% of the time, Pallas kernels for 0%

profile of v1, /device:TPU:8, one launch (start us, length us, event | category | flops | bytes accessed | tf_op | source)
XLA Modules:
  0.0 799.3 jit_solution(5134314741263809263)
XLA Ops:
  8.4 2.9 collective-permute-start.1
  16.8 2.9 collective-permute-start.3
  19.8 2.6 collective-permute-done.2
  22.4 3.0 collective-permute-start.5
  25.4 2.6 collective-permute-done.4
  28.5 6.0 collective-permute-done.6
  38.5 1.7 convolution_bitcast_fusion.5
  40.2 3.2 fusion.10
  44.0 3.2 fusion.8
  47.2 2.3 copy.52
  49.6 2.9 gather_fusion.3
  52.5 2.1 convolution_bitcast_fusion.2
  54.6 2.2 fusion.4
  59.6 3.2 multiply_convert_fusion.1
  64.7 3.2 multiply_convert_fusion.2
  69.6 3.3 multiply_convert_fusion
  75.1 3.0 fusion
  78.1 3.1 add_convert_fusion
  83.7 3.0 fusion.14
  88.2 192.3 %reduce-scatter.12.cloned.1.call-done = bf16[1,128,128]{2,1,0:T(8,128)(2,1)} async-done(((bf16[32,128,128]{2,1,0:T(8,128)(2,1)}), bf16[1,128,128]{2,1,0:T(8,128)(2,1)}) %reduce-scatter.12.cloned.1.call-update) | async-done | bytes 32784 | tf_op jit(solution)/shard_map/reduce_scatter | solution.py:117
  281.8 218.0 %reduce-scatter.10.cloned.1.call-done = bf16[1,128,128]{2,1,0:T(8,128)(2,1)} async-done(((bf16[32,128,128]{2,1,0:T(8,128)(2,1)}), bf16[1,128,128]{2,1,0:T(8,128)(2,1)}) %reduce-scatter.10.cloned.1.call-update) | async-done | bytes 32784 | tf_op jit(solution)/shard_map/reduce_scatter | solution.py:117
  501.2 217.8 %reduce-scatter.14.cloned.1.call-done = bf16[1,128,128]{2,1,0:T(8,128)(2,1)} async-done(((bf16[32,128,128]{2,1,0:T(8,128)(2,1)}), bf16[1,128,128]{2,1,0:T(8,128)(2,1)}) %reduce-scatter.14.cloned.1.call-update) | async-done | bytes 32784 | tf_op jit(solution)/shard_map/reduce_scatter | solution.py:117
  720.4 35.5 %reduce-scatter.8.cloned.1.call-done = bf16[128,512]{1,0:T(8,128)(2,1)} async-done(((bf16[128,4096]{1,0:T(8,128)(2,1)}), bf16[128,512]{1,0:T(8,128)(2,1)}) %reduce-scatter.8.cloned.1.call-update) | async-done | bytes 131088 | tf_op jit(solution)/shard_map/reduce_scatter | solution.py:122
  755.9 36.6 %reduce-scatter.6.cloned.1.call-done = bf16[128,512]{1,0:T(8,128)(2,1)} async-done(((bf16[128,4096]{1,0:T(8,128)(2,1)}), bf16[128,512]{1,0:T(8,128)(2,1)}) %reduce-scatter.6.cloned.1.call-update) | async-done | bytes 131088 | tf_op jit(solution)/shard_map/reduce_scatter | solution.py:93
  (83 shorter events, 28.0 us)
Async XLA Ops:
  7.2 36.3 %copy-start = (bf16[1,32,128,128]{3,2,1,0:T(8,128)(2,1)S(1)}, bf16[1,32,128,128]{3,2,1,0:T(8,128)(2,1)}, u32[]{:S(2)}) copy-start(bf16[1,32,128,128]{3,2,1,0:T(8,128)(2,1)} %param.17) | copy-start | bytes 3145732
  7.2 40.0 %all-gather.2.cloned.1.call-start = ((), (), s32[]{:S(2)}) async-start(), calls=%async_computation.6 | async-start | bytes 1179648 | tf_op jit(solution)/shard_map/all_gather | solution.py:67
  8.3 8.5 %collective-permute-start = (bf16[128,512]{0,1:T(8,128)(2,1)S(1)}, bf16[128,512]{0,1:T(8,128)(2,1)S(1)}, u32[]{:S(2)}, u32[]{:S(2)}) collective-permute-start(bf16[128,512]{0,1:T(8,128)(2,1)S(1)} %copy.41), channel_id=1, source_target_pairs={{0,1},{1,2},{2,3},{3,4},{4,5},{5,6},{6,7},{7,0},{8,9},{9,10},{10,1... | collective-permute-start | bytes 393224 | tf_op jit(solution)/shard_map/ppermute | solution.py:18
  8.4 8.5 %collective-permute-start.1 = (bf16[128,512]{0,1:T(8,128)(2,1)S(1)}, bf16[128,512]{0,1:T(8,128)(2,1)S(1)}, u32[]{:S(2)}, u32[]{:S(2)}) collective-permute-start(bf16[128,512]{0,1:T(8,128)(2,1)S(1)} %copy.41), channel_id=1, source_target_pairs={{0,7},{1,0},{2,1},{3,2},{4,3},{5,4},{6,5},{7,6},{8,15},{9,8},{10,9... | collective-permute-start | bytes 393224 | tf_op jit(solution)/shard_map/ppermute | solution.py:23
  13.0 267.4 %reduce-scatter.12.cloned.1.call-start = ((), (), s32[]{:S(2)}) async-start(), calls=%async_computation.9 | async-start | bytes 1081344 | tf_op jit(solution)/shard_map/reduce_scatter | solution.py:117
  16.8 5.6 collective-permute-start.2
  16.8 5.6 collective-permute-start.3
  22.4 5.6 collective-permute-start.4
  22.4 6.0 collective-permute-start.5
  28.0 6.5 collective-permute-start.6
  35.2 3.3 copy-start.1
  40.2 3.2 copy-start.7
  47.2 5.2 copy-start.2
  54.6 2.3 copy-start.8
  54.6 2.3 copy-start.9
  62.8 437.0 %reduce-scatter.10.cloned.1.call-start = ((), (), s32[]{:S(2)}) async-start(), calls=%async_computation.8 | async-start | bytes 1081344 | tf_op jit(solution)/shard_map/reduce_scatter | solution.py:117
  67.9 651.1 %reduce-scatter.14.cloned.1.call-start = ((), (), s32[]{:S(2)}) async-start(), calls=%async_computation.10 | async-start | bytes 1081344 | tf_op jit(solution)/shard_map/reduce_scatter | solution.py:117
  69.6 3.4 copy-start.4
  72.9 682.9 %reduce-scatter.8.cloned.1.call-start = ((), (), s32[]{:S(2)}) async-start(), calls=%async_computation.7 | async-start | bytes 1179648 | tf_op jit(solution)/shard_map/reduce_scatter | solution.py:122
  73.0 1.2 copy-start.6
  81.3 1.8 copy-start.3
  81.3 1.9 copy-start.5
  82.8 709.7 %reduce-scatter.6.cloned.1.call-start = ((), (), s32[]{:S(2)}) async-start(), calls=%async_computation.5 | async-start | bytes 1179648 | tf_op jit(solution)/shard_map/reduce_scatter | solution.py:93
Sparse Core Ops, SparseCore 0:
  13.1 27.4 all-gather.1
  62.9 217.4 reduce-scatter.11
  284.3 215.4 reduce-scatter.9
  503.5 215.4 reduce-scatter.13
  721.9 33.8 reduce-scatter.7
  758.8 33.5 reduce-scatter.5
